TPU v7x, 128 devices: a whole 4x4x4 slice. The times are simulated.
128 devices in a mesh: req: 8 (over z, core), wide: 16 (over y, x).
Axes of the slice: x: 4, y: 4, z: 4, core: 2. Of those that a mesh axis runs over, the one named last changes fastest.
Arguments:
- hidden_in: bfloat16 [16384, 2048], P(('req', 'wide')), may hold values from -6 to 6
- queries: bfloat16 [16384, 3072], P(('req', 'wide')), may hold values from -104 to 104
- latent_weight: bfloat16 [2048, 576], replicated, may hold values from -0.125 to 0.125
- latent_gain: float32 [512], replicated, may hold values from 0.25 to 1.75
- key_up: bfloat16 [512, 2048], replicated, may hold values from -0.25 to 0.25
- value_up: bfloat16 [512, 2048], replicated, may hold values from -2 to 2
- out_weight: bfloat16 [2048, 2048], replicated, may hold values from -0.5 to 0.5
- ffn_gain: float32 [2048], replicated, may hold values from 0.25 to 1.75
- router_weight: bfloat16 [2048, 64], replicated, may hold values from -0.046875 to 0.046875
- gate_pieces: bfloat16 [128, 2048, 704], P(('req', 'wide')), may hold values from -0.125 to 0.125
- up_pieces: bfloat16 [128, 2048, 704], P(('req', 'wide')), may hold values from -0.125 to 0.125
- down_pieces: bfloat16 [128, 704, 2048], P(('req', 'wide')), may hold values from -0.625 to 0.625
- prefix_latent: bfloat16 [8, 128, 512], P('req'), may hold values from -6 to 6
- prefix_rope: bfloat16 [8, 128, 64], P('req'), may hold values from -6 to 6
- page_table: int32 [8], replicated, may hold values from 0 to 7, each once
- segment_ids: int32 [8, 2048], P('req', 'wide'), may hold values from 0 to 7, never falling along the last dimension, each value on 1 to 1024 neighbouring positions
- expert_ids: int32 [16384, 6], P(('req', 'wide')), may hold values from 0 to 63, all different within a row; in each aligned block of 128 rows (0 to 127, 128 to 255, ...) at most 14 rows name the same one
Outputs:
- hidden_out: bfloat16 [16384, 2048], P(('req', 'wide'))
- suffix_cache: bfloat16 [16384, 576], P(('req', 'wide'))
Inputs may be any that keep to these rules, and one draw needn't show every extreme that they name: `segment_ids`: request numbers never fall along a row; each request holds 1 to 1024 tokens and one holds exactly 1024. `expert_ids`: A token names 6 different experts; among the 128 tokens of one device no expert is named more than 14 times, and that many is reached.
All inputs are finite; a program needn't handle non-finite values.
Results may differ from a plain program's by a relative error of at most 0.015.
Values may be sent and summed in bfloat16 or wider, within the bound.
No kernel may reach another device: no remote copies, remote signals or barrier semaphores. Data moves between devices by JAX's collectives and lax.ppermute only.
A program may use at most 192 MiB of HBM per device.

v0:
```python
import math

import jax
import jax.numpy as jnp
from jax import lax
from jax.sharding import PartitionSpec as P

D = 2048
HEADS = 16
NOPE = 128
ROPE = 64
LAT = 512
EXPERTS = 64
TOPK = 6
SPLIT = 2
PAGE = 128
CAP = 14


EPS = 1e-06
NEG = -1e30


def rotary(values, positions):
    half = values.shape[-1] // 2
    freqs = 10000.0 ** (-2.0 * jnp.arange(half, dtype=jnp.float32) / values.shape[-1])
    angles = positions.astype(jnp.float32)[:, None] * freqs[None, :]
    shape = (positions.shape[0],) + (1,) * (values.ndim - 2) + (half,)
    cosine = jnp.cos(angles).reshape(shape)
    sine = jnp.sin(angles).reshape(shape)
    first = values[..., :half]
    second = values[..., half:]
    return jnp.concatenate(
        [first * cosine - second * sine, second * cosine + first * sine], axis=-1
    )


def rms_scale(values, gain):
    return values * lax.rsqrt(jnp.mean(values * values, axis=-1, keepdims=True) + EPS) * gain


def offsets(segments):
    length = segments.shape[0]
    index = jnp.arange(length, dtype=jnp.int32)
    fresh = jnp.concatenate([jnp.ones((1,), dtype=bool), segments[1:] != segments[:-1]])
    starts = lax.cummax(jnp.where(fresh, index, 0), axis=0)
    return index - starts


def page_positions(page_table, slots):
    logical = jnp.sum(
        jnp.where(
            page_table[None, :] == slots[:, None],
            jnp.arange(page_table.shape[0], dtype=jnp.int32)[None, :],
            0,
        ),
        axis=1,
    )
    return (logical[:, None] * PAGE + jnp.arange(PAGE, dtype=jnp.int32)[None, :]).reshape(-1)


def expert_rows(received, gate_pieces, up_pieces, down_pieces):
    owned = gate_pieces.shape[0]
    grid = received.reshape(-1, owned, received.shape[1], received.shape[2])
    gate = jnp.einsum("spkd,pdf->spkf", grid, gate_pieces, preferred_element_type=jnp.float32)
    upper = jnp.einsum("spkd,pdf->spkf", grid, up_pieces, preferred_element_type=jnp.float32)
    active = (jax.nn.silu(gate) * upper).astype(jnp.bfloat16)
    output = jnp.einsum(
        "spkf,pfd->spkd", active, down_pieces, preferred_element_type=jnp.float32
    ).astype(jnp.bfloat16)
    return output.reshape(received.shape)


def on_device(
    hidden_in,
    queries,
    latent_weight,
    latent_gain,
    key_up,
    value_up,
    out_weight,
    ffn_gain,
    router_weight,
    gate_pieces,
    up_pieces,
    down_pieces,
    prefix_latent,
    prefix_rope,
    page_table,
    segment_ids,
    expert_ids,
):
    rows = hidden_in.shape[0]
    my_start = lax.axis_index("wide") * rows
    prefix_len = prefix_latent.shape[0] * lax.axis_size("req") * PAGE
    group_seg = lax.all_gather(segment_ids, "wide", axis=1, tiled=True)[0]
    seg_q = lax.dynamic_slice_in_dim(group_seg, my_start, rows, 0)
    index_q = my_start + jnp.arange(rows, dtype=jnp.int32)
    position = prefix_len + lax.dynamic_slice_in_dim(offsets(group_seg), my_start, rows, 0)
    raw = jnp.dot(hidden_in, latent_weight, preferred_element_type=jnp.float32)
    latent = rms_scale(raw[:, :LAT], latent_gain).astype(jnp.bfloat16)
    key_rope = raw[:, LAT:].astype(jnp.bfloat16)
    suffix_cache = jnp.concatenate([latent, key_rope], axis=1)
    suffix_rot = rotary(key_rope.astype(jnp.float32), position).astype(jnp.bfloat16)
    split_q = queries.reshape(rows, HEADS, NOPE + ROPE)
    q_lat = jnp.einsum(
        "thn,lhn->thl",
        split_q[..., :NOPE],
        key_up.reshape(LAT, HEADS, NOPE),
        preferred_element_type=jnp.float32,
    ).astype(jnp.bfloat16)
    q_rot = rotary(split_q[..., NOPE:].astype(jnp.float32), position).astype(jnp.bfloat16)
    scale = 1.0 / math.sqrt(NOPE + ROPE)

    def absorb(carry, keys_lat, keys_rot, allowed):
        best, total, accum = carry
        scores = (
            jnp.einsum("thl,kl->thk", q_lat, keys_lat, preferred_element_type=jnp.float32)
            + jnp.einsum("the,ke->thk", q_rot, keys_rot, preferred_element_type=jnp.float32)
        ) * scale
        if allowed is not None:
            scores = jnp.where(allowed[:, None, :], scores, NEG)
        fresh = jnp.maximum(best, jnp.max(scores, axis=-1))
        factor = jnp.exp(best - fresh)
        weights = jnp.exp(scores - fresh[..., None])
        total = total * factor + jnp.sum(weights, axis=-1)
        accum = accum * factor[..., None] + jnp.einsum(
            "thk,kl->thl",
            weights.astype(jnp.bfloat16),
            keys_lat,
            preferred_element_type=jnp.float32,
        )
        return (fresh, total, accum)

    initial = (
        jnp.full((rows, HEADS), NEG, jnp.float32),
        jnp.zeros((rows, HEADS), jnp.float32),
        jnp.zeros((rows, HEADS, LAT), jnp.float32),
    )
    page_lat = lax.all_gather(prefix_latent, "req", axis=0, tiled=True)
    page_rope = lax.all_gather(prefix_rope, "req", axis=0, tiled=True)
    count = page_lat.shape[0]
    slots = jnp.arange(count, dtype=jnp.int32)
    key_pos = page_positions(page_table, slots)
    keys_rot = rotary(page_rope.reshape(-1, ROPE).astype(jnp.float32), key_pos).astype(jnp.bfloat16)
    carry = absorb(initial, page_lat.reshape(-1, LAT), keys_rot, None)
    group_lat = lax.all_gather(latent, "wide", axis=0, tiled=True)
    group_rot = lax.all_gather(suffix_rot, "wide", axis=0, tiled=True)
    count = group_lat.shape[0]
    index_k = jnp.arange(count, dtype=jnp.int32)
    allowed = (seg_q[:, None] == group_seg[None, :]) & (index_k[None, :] <= index_q[:, None])
    carry = lax.cond(
        jnp.int32(0) <= my_start + rows - 1,
        lambda state: absorb(state, group_lat, group_rot, allowed),
        lambda state: state,
        carry,
    )
    best, total, accum = carry
    mixed = (accum / total[..., None]).astype(jnp.bfloat16)
    head_out = (
        jnp.einsum(
            "thl,lhn->thn",
            mixed,
            value_up.reshape(LAT, HEADS, NOPE),
            preferred_element_type=jnp.float32,
        )
        .astype(jnp.bfloat16)
        .reshape(rows, HEADS * NOPE)
    )
    residual = hidden_in.astype(jnp.float32) + jnp.dot(
        head_out, out_weight, preferred_element_type=jnp.float32
    )
    normed = rms_scale(residual, ffn_gain).astype(jnp.bfloat16)
    logits = jnp.dot(normed, router_weight, preferred_element_type=jnp.float32)
    hits = expert_ids[..., None] == jnp.arange(EXPERTS, dtype=jnp.int32)
    chosen = jnp.sum(jnp.where(hits, logits[:, None, :], 0.0), axis=-1)
    gates = jax.nn.softmax(chosen, axis=-1)
    flat_hits = hits.reshape(rows * TOPK, EXPERTS).astype(jnp.int32)
    slot = jnp.sum((jnp.cumsum(flat_hits, axis=0) - flat_hits) * flat_hits, axis=-1).reshape(
        rows, TOPK
    )
    target = expert_ids * CAP + slot
    selector = jnp.any(
        target[None, :, :] == jnp.arange(EXPERTS * CAP, dtype=jnp.int32)[:, None, None], axis=-1
    ).astype(jnp.bfloat16)
    packed = (
        jnp.dot(selector, normed, preferred_element_type=jnp.float32)
        .astype(jnp.bfloat16)
        .reshape(EXPERTS, 1, CAP, D)
    )
    outgoing = jnp.broadcast_to(packed, (EXPERTS, SPLIT, CAP, D)).reshape(EXPERTS * SPLIT, CAP, D)
    worked = expert_rows(
        lax.all_to_all(outgoing, ("req", "wide"), split_axis=0, concat_axis=0, tiled=True),
        gate_pieces,
        up_pieces,
        down_pieces,
    )
    returned = lax.all_to_all(worked, ("req", "wide"), split_axis=0, concat_axis=0, tiled=True)
    halves = jnp.sum(returned.reshape(EXPERTS, SPLIT, CAP, D).astype(jnp.float32), axis=1).reshape(
        EXPERTS * CAP, D
    )
    picked = jnp.take(halves, target.reshape(-1), axis=0).reshape(rows, TOPK, D)
    routed = jnp.sum(gates[..., None] * picked, axis=1)
    return ((residual + routed).astype(jnp.bfloat16), suffix_cache)


def solution(mesh):
    return jax.shard_map(
        on_device,
        mesh=mesh,
        in_specs=(
            P(("req", "wide"), None),
            P(("req", "wide"), None),
            P(),
            P(),
            P(),
            P(),
            P(),
            P(),
            P(),
            P(("req", "wide"), None, None),
            P(("req", "wide"), None, None),
            P(("req", "wide"), None, None),
            P("req", None, None),
            P("req", None, None),
            P(),
            P("req", "wide"),
            P(("req", "wide"), None),
        ),
        out_specs=(P(("req", "wide"), None), P(("req", "wide"), None)),
        check_vma=False,
    )
```

profile of v0, /device:TPU:5, one launch (start us, length us, event | category | flops | bytes accessed | tf_op | source)
XLA Modules:
  0.0 490.0 jit_solution(262791157175028469)
XLA Ops:
  8.0 2.7 fusion.69
  10.8 1.5 multiply_convert_fusion.1
  12.9 0.8 copy.99
  14.0 16.0 %all_gather.16 = s32[1,2048]{1,0:T(1,128)S(1)} all-gather(s32[1,128]{1,0:T(1,128)} %param.34), channel_id=1, replica_groups=mesh['req'=8,'wide'=16] {'wide'}, dimensions={1}, use_global_device_ids=true | all-gather | bytes 8704 | tf_op jit(solution)/shard_map/all_gather | solution.py:96
  30.7 2.3 copy.90
  33.0 1.0 slice_convert_fusion
  34.9 0.8 subtract_convert_fusion.1
  35.7 19.1 %all_gather.19 = bf16[2048,64]{0,1:T(8,128)(2,1)} all-gather(bf16[128,64]{0,1:T(8,128)(2,1)S(1)} %pad_maximum_fusion.2), channel_id=1, replica_groups=mesh['req'=8,'wide'=16] {'wide'}, dimensions={0}, use_global_device_ids=true | all-gather | bytes 278528 | tf_op jit(solution)/shard_map/all_gather | solution.py:148
  54.7 3.9 copy.114
  59.4 4.4 reduce-window.19
  63.8 1.2 slice_reduce_fusion
  65.0 1.1 fusion.44
  66.9 0.8 subtract_convert_fusion
  68.4 24.4 %all_gather.17 = bf16[8,128,64]{1,2,0:T(8,128)(2,1)S(1)} all-gather(bf16[1,128,64]{1,2,0:T(8,128)(2,1)} %param.32), channel_id=1, replica_groups=mesh['req'=8,'wide'=16] {'req'}, dimensions={0}, use_global_device_ids=true | all-gather | bytes 147456 | tf_op jit(solution)/shard_map/all_gather | solution.py:141
  92.8 1.1 fusion.29
  93.9 1.2 fusion.51
  95.2 3.8 convert_bitcast_fusion
  98.9 4.3 fusion.68
  103.3 1.4 fusion.67
  104.7 2.1 fusion.14
  106.9 4.1 broadcast_add_fusion
  110.9 1.1 le.37
  112.0 44.9 %conditional.1 = ((f32[128,16]{0,1:T(8,128)S(1)}, f32[128,16,512]{2,0,1:T(8,128)})) conditional(s32[]{:T(128)} %convert_element_type.94, (f32[128,16]{0,1:T(8,128)S(1)}, f32[128,16,512]{2,0,1:T(8,128)}) %tuple.17, (s32[1,2048]{1,0:T(1,128)S(1)}, s32[]{:T(128)}, s32[]{:T(128)}, s32[128,1]{0,1:T(1,128)S(1)}, s32[128,2048]{1,0:T(8,128)}, ...), branch_computations={%region_6.7_spmd, %region_7.10_spmd} | conditional | flops 9163247616 | bytes 100789280 | solution.py:152
  112.1 1.5 compare_and_fusion
  113.6 12.5 %fusion.5 = f32[128,16,2048]{2,0,1:T(8,128)} fusion(bf16[128,16,512]{0,2,1:T(8,128)(2,1)} %get-tuple-element.139, bf16[2048,512]{0,1:T(8,128)(2,1)} %get-tuple-element.140), kind=kOutput, calls=%fused_computation.8 | convolution fusion | flops 4294967296 | bytes 20971520 | tf_op jit(solution)/shard_map/cond/branch_1_fun/thl,kl->thk/dot_general | solution.py:118
  126.1 10.9 %fusion.66 = (f32[128,16]{0,1:T(8,128)S(1)}, f32[128,16,2048]{2,0,1:T(8,128)}) fusion(f32[128,16,2048]{2,0,1:T(8,128)} %fusion.5, bf16[128,16,64]{0,2,1:T(8,128)(2,1)S(1)} %get-tuple-element.77, bf16[2048,64]{0,1:T(8,128)(2,1)S(1)} %get-tuple-element.78, pred[128,2048]{1,0:T(8,128)(4,1)S(1)} %compare_and_fusion), kind=kOutput, calls=%fused_computation.127 | convolution fusion | flops 553646080 | bytes 34349056 | tf_op jit(solution)/shard_map/cond/branch_1_fun/the,ke->thk/dot_general | solution.py:119
  137.0 8.1 %fusion.1 = f32[128,16]{0,1:T(8,128)S(1)} fusion(f32[128,16,2048]{2,0,1:T(8,128)} %get-tuple-element.153, f32[128,16]{0,1:T(8,128)S(1)} %max.3), kind=kLoop, calls=%fused_computation.4 | loop fusion | flops 8386560 | bytes 16793600 | tf_op jit(solution)/shard_map/cond/branch_1_fun/reduce_sum | solution.py:126
  145.2 11.7 %multiply_add_fusion = f32[128,16,512]{2,0,1:T(8,128)} fusion(f32[128,16,512]{2,0,1:T(8,128)} %get-tuple-element.79, f32[128,16]{0,1:T(8,128)S(1)} %get-tuple-element.147, bf16[2048,512]{0,1:T(8,128)(2,1)} %get-tuple-element.140, f32[128,16,2048]{2,0,1:T(8,128)} %get-tuple-element.153, f32[128,16]{0,1:T(8,128)S(1)} %max.3), kind=kOutput, calls=%fused_computation.7 | convolution fusion | flops 4305453056 | bytes 27279360 | tf_op jit(solution)/shard_map/cond/branch_1_fun/thk,kl->thl/dot_general | solution.py:127
  156.9 3.7 fusion.40
  160.7 4.8 multiply_reduce_fusion.1
  165.5 1.0 copy-done.1
  166.5 3.0 convolution_convert_fusion.1
  169.4 5.9 %broadcast_in_dim.68 = bf16[64,14,2048]{2,1,0:T(8,128)(2,1)} reshape(bf16[896,2048]{1,0:T(8,128)(2,1)} %convolution_convert_fusion.1) | data formatting | bytes 7340032 | tf_op jit(solution)/shard_map/broadcast_in_dim | solution.py:191
  175.3 6.8 %broadcast_in_dim.72 = bf16[64,2,14,2048]{3,2,1,0:T(8,128)(2,1)} broadcast(bf16[64,14,2048]{2,1,0:T(8,128)(2,1)} %broadcast_in_dim.68), dimensions={0,2,3} | broadcast | bytes 11010048 | tf_op jit(solution)/shard_map/broadcast_in_dim | solution.py:191
  182.1 103.9 %all_to_all.10 = bf16[128,14,2048]{2,1,0:T(8,128)(2,1)S(1)} all-to-all(bf16[128,14,2048]{2,1,0:T(8,128)(2,1)} %bitcast.136), channel_id=1, replica_groups=mesh['req'=8,'wide'=16] {'req','wide'}, dimensions={0} | all-to-all | bytes 14680064 | tf_op jit(solution)/shard_map/all_to_all | solution.py:193
  286.0 10.7 %fusion.15 = f32[128,14,704]{0,2,1:T(8,128)S(1)} fusion(bf16[128,14,2048]{2,1,0:T(8,128)(2,1)S(1)} %all_to_all.10, bf16[1,2048,704]{1,2,0:T(8,128)(2,1)S(1)} %copy-done.15), kind=kOutput, calls=%fused_computation.23 | convolution fusion | flops 5167382528 | bytes 15269888 | tf_op jit(solution)/shard_map/spkd,pdf->spkf/dot_general | solution.py:66
  296.7 10.9 %fusion.17 = f32[128,14,704]{0,2,1:T(8,128)S(1)} fusion(bf16[128,14,2048]{2,1,0:T(8,128)(2,1)S(1)} %all_to_all.10, bf16[1,2048,704]{1,2,0:T(8,128)(2,1)S(1)} %copy-done.16), kind=kOutput, calls=%fused_computation.25 | convolution fusion | flops 5167382528 | bytes 15269888 | tf_op jit(solution)/shard_map/spkd,pdf->spkf/dot_general | solution.py:65
  307.6 8.4 %convolution_convert_fusion = bf16[128,14,2048]{2,0,1:T(8,128)(2,1)} fusion(bf16[1,704,2048]{2,1,0:T(8,128)(2,1)S(1)} %copy-done, f32[128,14,704]{0,2,1:T(8,128)S(1)} %fusion.15, f32[128,14,704]{0,2,1:T(8,128)S(1)} %fusion.17), kind=kOutput, calls=%fused_computation.34 | convolution fusion | flops 5178621952 | bytes 20316160 | tf_op jit(solution)/shard_map/spkf,pfd->spkd/dot_general | solution.py:68
  316.0 10.4 %copy.106 = bf16[128,14,2048]{2,1,0:T(8,128)(2,1)} copy(bf16[128,14,2048]{2,0,1:T(8,128)(2,1)} %convolution_convert_fusion) | data formatting | bytes 14680064 | tf_op jit(solution)/shard_map/convert_element_type | solution.py:70
  326.4 5.9 %all-to-all-start.1 = ((bf16[128,14,2048]{2,1,0:T(8,128)(2,1)}), bf16[128,14,2048]{2,1,0:T(8,128)(2,1)}, u32[]{:S(2)}, u32[]{:S(2)}) async-start(bf16[128,14,2048]{2,1,0:T(8,128)(2,1)} %copy.106), calls=%async_computation.1 | async-start | bytes 16777216 | tf_op jit(solution)/shard_map/all_to_all | solution.py:198
  333.5 1.6 fusion.64
  335.3 103.8 %all-to-all-done.1 = bf16[128,14,2048]{2,1,0:T(8,128)(2,1)} async-done(((bf16[128,14,2048]{2,1,0:T(8,128)(2,1)}), bf16[128,14,2048]{2,1,0:T(8,128)(2,1)}, u32[]{:S(2)}, u32[]{:S(2)}) %all-to-all-start.1) | async-done | bytes 7340064 | tf_op jit(solution)/shard_map/all_to_all | solution.py:198
  439.1 9.8 %convert_reduce_fusion = f32[64,14,2048]{2,1,0:T(8,128)} fusion(bf16[128,14,2048]{2,1,0:T(8,128)(2,1)} %all-to-all-done.1), kind=kLoop, calls=%fused_computation.17 | loop fusion | flops 5505024 | bytes 14680064 | tf_op jit(solution)/shard_map/reduce_sum | solution.py:199
  448.9 8.2 %reshape.291 = f32[896,2048]{1,0:T(8,128)} reshape(f32[64,14,2048]{2,1,0:T(8,128)} %convert_reduce_fusion) | data formatting | bytes 14680064 | tf_op jit(solution)/shard_map/reshape | solution.py:199
  457.1 10.3 %gather_fusion = f32[768,2048]{1,0:T(8,128)} fusion(f32[896,2048]{1,0:T(8,128)} %reshape.291, s32[1024]{0:T(1024)S(1)} %pad_clamp_fusion), kind=kCustom, calls=%fused_computation | custom fusion | bytes 12585984 | tf_op jit(solution)/shard_map/jit(_take)/gather | solution.py:202
  467.4 7.8 %gather.7 = f32[128,6,2048]{2,1,0:T(8,128)} reshape(f32[768,2048]{1,0:T(8,128)} %gather_fusion) | data formatting | bytes 12582912 | tf_op jit(solution)/shard_map/jit(_take)/gather | solution.py:202
  475.2 6.6 %multiply_reduce_fusion = f32[128,2048]{1,0:T(8,128)S(1)} fusion(f32[128,6,2048]{2,1,0:T(8,128)} %gather.7, f32[128,6]{1,0:T(8,128)S(1)} %copy.98, pred[128,6]{1,0:T(8,128)(4,1)S(1)} %copy.103), kind=kLoop, calls=%fused_computation.18 | loop fusion | flops 4456448 | bytes 7343872 | tf_op jit(solution)/shard_map/reduce_sum | solution.py:203
  481.8 0.9 add_convert_fusion
  (87 shorter events, 7.1 us)
Async XLA Ops:
  7.2 300.4 %copy-start = (bf16[1,704,2048]{2,1,0:T(8,128)(2,1)S(1)}, bf16[1,704,2048]{2,1,0:T(8,128)(2,1)}, u32[]{:S(2)}) copy-start(bf16[1,704,2048]{2,1,0:T(8,128)(2,1)} %param.30) | copy-start | bytes 8650756
  7.2 26.9 %copy-start.18 = (s32[8]{0:T(128)S(1)}, s32[8]{0:T(128)}, u32[]{:S(2)}) copy-start(s32[8]{0:T(128)} %param.33) | copy-start | bytes 100
  7.2 91.7 %all-gather.3.cloned.1.call-start = ((), (), s32[]{:S(2)}) async-start(), calls=%async_computation.2 | async-start | bytes 1179648 | tf_op jit(solution)/shard_map/all_gather | solution.py:140
  7.9 103.0 %all-gather.5.cloned.1.call-start = ((), (), s32[]{:S(2)}) async-start(), calls=%async_computation.3 | async-start | bytes 2228224 | tf_op jit(solution)/shard_map/all_gather | solution.py:147
  10.7 55.6 %copy-start.11 = (s32[128,6]{0,1:T(8,128)S(1)}, s32[128,6]{0,1:T(8,128)}, u32[]{:S(2)}) copy-start(s32[128,6]{0,1:T(8,128)} %param.35) | copy-start | bytes 9220
  12.9 54.0 %copy-start.14 = (f32[32]{0:T(128)}, f32[32]{0:T(128)S(1)}, u32[]{:S(2)}) copy-start(f32[32]{0:T(128)S(1)} %multiply_power_fusion) | copy-start | bytes 388
  67.7 0.7 copy-start.4
  98.9 4.3 copy-start.5
  104.7 2.2 copy-start.17
  106.8 5.2 %copy-start.7 = (bf16[2048,64]{0,1:T(8,128)(2,1)S(1)}, bf16[2048,64]{0,1:T(8,128)(2,1)}, u32[]{:S(2)}) copy-start(bf16[2048,64]{0,1:T(8,128)(2,1)} %all_gather.19) | copy-start | bytes 786436
  156.9 3.7 copy-start.3
  160.6 5.8 %copy-start.8 = (pred[896,128]{1,0:T(8,128)(4,1)S(1)}, pred[896,128]{1,0:T(8,128)(4,1)}, u32[]{:S(2)}) copy-start(pred[896,128]{1,0:T(8,128)(4,1)} %fusion.29) | copy-start | bytes 344068
  160.6 5.8 %copy-start.12 = (f32[2048]{0:T(1024)S(1)}, f32[2048]{0:T(1024)}, u32[]{:S(2)}) copy-start(f32[2048]{0:T(1024)} %param.26) | copy-start | bytes 24580
  165.4 1.0 copy-start.1
  182.1 103.9 %copy-start.15 = (bf16[1,2048,704]{1,2,0:T(8,128)(2,1)S(1)}, bf16[1,2048,704]{1,2,0:T(8,128)(2,1)}, u32[]{:S(2)}) copy-start(bf16[1,2048,704]{1,2,0:T(8,128)(2,1)} %param.29) | copy-start | bytes 8650756
  286.0 10.7 %copy-start.16 = (bf16[1,2048,704]{1,2,0:T(8,128)(2,1)S(1)}, bf16[1,2048,704]{1,2,0:T(8,128)(2,1)}, u32[]{:S(2)}) copy-start(bf16[1,2048,704]{1,2,0:T(8,128)(2,1)} %param.28) | copy-start | bytes 8650756
  326.4 6.2 %copy-start.13 = (pred[128,6]{0,1:T(8,128)(4,1)S(1)}, pred[128,6]{0,1:T(8,128)(4,1)}, u32[]{:S(2)}) copy-start(pred[128,6]{0,1:T(8,128)(4,1)} %get-tuple-element.148) | copy-start | bytes 2308
  326.4 6.3 %copy-start.6 = (bf16[128,512]{0,1:T(8,128)(2,1)S(1)}, bf16[128,512]{0,1:T(8,128)(2,1)}, u32[]{:S(2)}) copy-start(bf16[128,512]{0,1:T(8,128)(2,1)} %multiply_convert_fusion.1) | copy-start | bytes 393220
  326.4 6.4 %copy-start.10 = (bf16[128,64]{0,1:T(8,128)(2,1)S(1)}, bf16[128,64]{0,1:T(8,128)(2,1)}, u32[]{:S(2)}) copy-start(bf16[128,64]{0,1:T(8,128)(2,1)} %get-tuple-element.151) | copy-start | bytes 49156
  326.4 7.0 %copy-start.9 = (bf16[2048,64]{0,1:T(8,128)(2,1)S(1)}, bf16[2048,64]{0,1:T(8,128)(2,1)}, u32[]{:S(2)}) copy-start(bf16[2048,64]{0,1:T(8,128)(2,1)} %param.27) | copy-start | bytes 786436
  326.4 112.6 %all-to-all-start.1 = ((bf16[128,14,2048]{2,1,0:T(8,128)(2,1)}), bf16[128,14,2048]{2,1,0:T(8,128)(2,1)}, u32[]{:S(2)}, u32[]{:S(2)}) async-start(bf16[128,14,2048]{2,1,0:T(8,128)(2,1)} %copy.106), calls=%async_computation.1 | async-start | bytes 16777216 | tf_op jit(solution)/shard_map/all_to_all | solution.py:198
  475.2 6.6 %copy-start.2 = (f32[128,2048]{1,0:T(8,128)S(1)}, f32[128,2048]{1,0:T(8,128)}, u32[]{:S(2)}) copy-start(f32[128,2048]{1,0:T(8,128)} %copy-done.1) | copy-start | bytes 3145732
Sparse Core Ops, SparseCore 0:
  9.7 26.3 all-gather.2
  38.3 44.7 all-gather.4
where the time goes:
time: 498 us; the launch traced here: 490 us
  blocking collectives  163 us (33%)
  waiting for transfers between devices  104 us (21%)
  matrix products  94.5 us (19%)
  local copies, waits for them, and re-layouts  61.6 us (12%)
  other arithmetic  45.2 us (9%)
  between operations  14.8 us (3%)
  starting transfers between devices  5.97 us (1%)
    all_to_all x1, blocking collectives, on_device(): lax.all_to_all(outgoing, ('req', 'wide'), split_axis=0, concat_axis=0, ti...  104 us
    all_to_all x1, waiting for transfers between devices, on_device(): lax.all_to_all(worked, ('req', 'wide'), split_axis=0, concat_axis=0, tile...  104 us
    all_gather x1, blocking collectives, on_device(): page_rope = lax.all_gather(prefix_rope, 'req', axis=0, tiled=True)  24.4 us
    all_gather x1, blocking collectives, on_device(): group_rot = lax.all_gather(suffix_rot, 'wide', axis=0, tiled=True)  19.1 us
    gather x2, local copies, waits for them, and re-layouts, on_device(): picked = jnp.take(halves, target.reshape(-1), axis=0).reshape(rows, TOPK, D)  18.2 us
    dot_general x2, matrix products, absorb(): jnp.einsum('thl,kl->thk', q_lat, keys_lat, preferred_element_type=jnp.flo...  16.8 us
    all_gather x1, blocking collectives, on_device(): group_seg = lax.all_gather(segment_ids, 'wide', axis=1, tiled=True)[0]  16 us
    dot_general x2, matrix products, absorb(): jnp.einsum('thk,kl->thl', weights.astype(jnp.bfloat16), keys_lat, preferr...  15.8 us
  transfers between devices with their start and end apart: 3, of which 1 were waited for; matrix products, arithmetic and copies ran while one was open for 9% of the time, Pallas kernels for 0%

commit v1 on v0

--- a/solution.py
+++ b/solution.py
@@ -1,8 +1,11 @@
+import functools
 import math
 
 import jax
 import jax.numpy as jnp
 from jax import lax
+from jax.experimental import pallas as pl
+from jax.experimental.pallas import tpu as pltpu
 from jax.sharding import PartitionSpec as P
 
 D = 2048
@@ -15,6 +18,7 @@
 SPLIT = 2
 PAGE = 128
 CAP = 14
+MOST_LEN = 1024
 
 
 EPS = 1e-06
@@ -57,6 +61,48 @@
         axis=1,
     )
     return (logical[:, None] * PAGE + jnp.arange(PAGE, dtype=jnp.int32)[None, :]).reshape(-1)
+
+
+def attend_kernel(base_ref, q_ref, kp_ref, ks_ref, lo_ref, hi_ref, out_ref, *, window, scale):
+    base = pl.multiple_of(base_ref[0], 128)
+    q = q_ref[...]
+    kp = kp_ref[...]
+    ks = ks_ref[pl.ds(base, window), :]
+    dims = (((1,), (1,)), ((), ()))
+    s_p = lax.dot_general(q, kp, dims, preferred_element_type=jnp.float32) * scale
+    s_s = lax.dot_general(q, ks, dims, preferred_element_type=jnp.float32) * scale
+    kidx = base + lax.broadcasted_iota(jnp.int32, (1, window), 1)
+    allowed = (kidx >= lo_ref[...]) & (kidx <= hi_ref[...])
+    s_s = jnp.where(allowed, s_s, NEG)
+    top = jnp.maximum(jnp.max(s_p, axis=1, keepdims=True), jnp.max(s_s, axis=1, keepdims=True))
+    w_p = jnp.exp(s_p - top)
+    w_s = jnp.exp(s_s - top)
+    total = jnp.sum(w_p, axis=1, keepdims=True) + jnp.sum(w_s, axis=1, keepdims=True)
+    accum = jnp.dot(w_p.astype(jnp.bfloat16), kp, preferred_element_type=jnp.float32) + jnp.dot(
+        w_s.astype(jnp.bfloat16), ks, preferred_element_type=jnp.float32
+    )
+    lat = out_ref.shape[1]
+    out_ref[...] = (accum[:, :lat] / total).astype(out_ref.dtype)
+
+
+def attend(base, q, kp, ks, lo, hi, window, block=256):
+    rows, width = q.shape
+    return pl.pallas_call(
+        functools.partial(attend_kernel, window=window, scale=1.0 / math.sqrt(NOPE + ROPE)),
+        grid_spec=pltpu.PrefetchScalarGridSpec(
+            num_scalar_prefetch=1,
+            grid=(rows // block,),
+            in_specs=[
+                pl.BlockSpec((block, width), lambda i, b: (i, 0)),
+                pl.BlockSpec(kp.shape, lambda i, b: (0, 0)),
+                pl.BlockSpec(ks.shape, lambda i, b: (0, 0)),
+                pl.BlockSpec((block, 1), lambda i, b: (i, 0)),
+                pl.BlockSpec((block, 1), lambda i, b: (i, 0)),
+            ],
+            out_specs=pl.BlockSpec((block, LAT), lambda i, b: (i, 0)),
+        ),
+        out_shape=jax.ShapeDtypeStruct((rows, LAT), jnp.bfloat16),
+    )(base, q, kp, ks, lo, hi)
 
 
 def expert_rows(received, gate_pieces, up_pieces, down_pieces):
@@ -91,17 +137,29 @@
     expert_ids,
 ):
     rows = hidden_in.shape[0]
-    my_start = lax.axis_index("wide") * rows
+    n_wide = lax.axis_size("wide")
+    wide_at = lax.axis_index("wide")
+    my_start = wide_at * rows
     prefix_len = prefix_latent.shape[0] * lax.axis_size("req") * PAGE
+    slots = lax.axis_index("req") * prefix_latent.shape[0] + jnp.arange(
+        prefix_latent.shape[0], dtype=jnp.int32
+    )
+    key_pos = page_positions(page_table, slots)
+    own_rot = rotary(prefix_rope.reshape(-1, ROPE).astype(jnp.float32), key_pos).astype(jnp.bfloat16)
+    own_keys = jnp.concatenate([prefix_latent.reshape(-1, LAT), own_rot], axis=1)
+    page_keys = lax.all_gather(own_keys, "req", axis=0, tiled=True)
     group_seg = lax.all_gather(segment_ids, "wide", axis=1, tiled=True)[0]
-    seg_q = lax.dynamic_slice_in_dim(group_seg, my_start, rows, 0)
     index_q = my_start + jnp.arange(rows, dtype=jnp.int32)
-    position = prefix_len + lax.dynamic_slice_in_dim(offsets(group_seg), my_start, rows, 0)
+    offs = lax.dynamic_slice_in_dim(offsets(group_seg), my_start, rows, 0)
+    position = prefix_len + offs
     raw = jnp.dot(hidden_in, latent_weight, preferred_element_type=jnp.float32)
     latent = rms_scale(raw[:, :LAT], latent_gain).astype(jnp.bfloat16)
     key_rope = raw[:, LAT:].astype(jnp.bfloat16)
     suffix_cache = jnp.concatenate([latent, key_rope], axis=1)
     suffix_rot = rotary(key_rope.astype(jnp.float32), position).astype(jnp.bfloat16)
+    group_keys = lax.all_gather(
+        jnp.concatenate([latent, suffix_rot], axis=1), "wide", axis=0, tiled=True
+    )
     split_q = queries.reshape(rows, HEADS, NOPE + ROPE)
     q_lat = jnp.einsum(
         "thn,lhn->thl",
@@ -110,53 +168,15 @@
         preferred_element_type=jnp.float32,
     ).astype(jnp.bfloat16)
     q_rot = rotary(split_q[..., NOPE:].astype(jnp.float32), position).astype(jnp.bfloat16)
-    scale = 1.0 / math.sqrt(NOPE + ROPE)
-
-    def absorb(carry, keys_lat, keys_rot, allowed):
-        best, total, accum = carry
-        scores = (
-            jnp.einsum("thl,kl->thk", q_lat, keys_lat, preferred_element_type=jnp.float32)
-            + jnp.einsum("the,ke->thk", q_rot, keys_rot, preferred_element_type=jnp.float32)
-        ) * scale
-        if allowed is not None:
-            scores = jnp.where(allowed[:, None, :], scores, NEG)
-        fresh = jnp.maximum(best, jnp.max(scores, axis=-1))
-        factor = jnp.exp(best - fresh)
-        weights = jnp.exp(scores - fresh[..., None])
-        total = total * factor + jnp.sum(weights, axis=-1)
-        accum = accum * factor[..., None] + jnp.einsum(
-            "thk,kl->thl",
-            weights.astype(jnp.bfloat16),
-            keys_lat,
-            preferred_element_type=jnp.float32,
-        )
-        return (fresh, total, accum)
-
-    initial = (
-        jnp.full((rows, HEADS), NEG, jnp.float32),
-        jnp.zeros((rows, HEADS), jnp.float32),
-        jnp.zeros((rows, HEADS, LAT), jnp.float32),
-    )
-    page_lat = lax.all_gather(prefix_latent, "req", axis=0, tiled=True)
-    page_rope = lax.all_gather(prefix_rope, "req", axis=0, tiled=True)
-    count = page_lat.shape[0]
-    slots = jnp.arange(count, dtype=jnp.int32)
-    key_pos = page_positions(page_table, slots)
-    keys_rot = rotary(page_rope.reshape(-1, ROPE).astype(jnp.float32), key_pos).astype(jnp.bfloat16)
-    carry = absorb(initial, page_lat.reshape(-1, LAT), keys_rot, None)
-    group_lat = lax.all_gather(latent, "wide", axis=0, tiled=True)
-    group_rot = lax.all_gather(suffix_rot, "wide", axis=0, tiled=True)
-    count = group_lat.shape[0]
-    index_k = jnp.arange(count, dtype=jnp.int32)
-    allowed = (seg_q[:, None] == group_seg[None, :]) & (index_k[None, :] <= index_q[:, None])
-    carry = lax.cond(
-        jnp.int32(0) <= my_start + rows - 1,
-        lambda state: absorb(state, group_lat, group_rot, allowed),
-        lambda state: state,
-        carry,
-    )
-    best, total, accum = carry
-    mixed = (accum / total[..., None]).astype(jnp.bfloat16)
+    q_all = jnp.concatenate([q_lat, q_rot], axis=2).reshape(rows * HEADS, LAT + ROPE)
+    reach = -(-(MOST_LEN - 1) // rows) + 1
+    blocks = min(n_wide, reach)
+    base = (jnp.maximum(wide_at - (blocks - 1), 0) * rows).astype(jnp.int32).reshape(1)
+    lo = jnp.repeat((index_q - offs)[:, None], HEADS, axis=0)
+    hi = jnp.repeat(index_q[:, None], HEADS, axis=0)
+    mixed = attend(base, q_all, page_keys, group_keys, lo, hi, blocks * rows).reshape(
+        rows, HEADS, LAT
+    )
     head_out = (
         jnp.einsum(
             "thl,lhn->thn",
@@ -179,16 +199,17 @@
     slot = jnp.sum((jnp.cumsum(flat_hits, axis=0) - flat_hits) * flat_hits, axis=-1).reshape(
         rows, TOPK
     )
-    target = expert_ids * CAP + slot
-    selector = jnp.any(
-        target[None, :, :] == jnp.arange(EXPERTS * CAP, dtype=jnp.int32)[:, None, None], axis=-1
-    ).astype(jnp.bfloat16)
-    packed = (
+    column = jnp.arange(EXPERTS * SPLIT * CAP, dtype=jnp.int32)
+    first = expert_ids * (SPLIT * CAP) + slot
+    match = jnp.zeros((EXPERTS * SPLIT * CAP, rows, TOPK), dtype=bool)
+    for half in range(SPLIT):
+        match = match | ((first + half * CAP)[None, :, :] == column[:, None, None])
+    selector = jnp.any(match, axis=-1).astype(jnp.bfloat16)
+    outgoing = (
         jnp.dot(selector, normed, preferred_element_type=jnp.float32)
         .astype(jnp.bfloat16)
-        .reshape(EXPERTS, 1, CAP, D)
-    )
-    outgoing = jnp.broadcast_to(packed, (EXPERTS, SPLIT, CAP, D)).reshape(EXPERTS * SPLIT, CAP, D)
+        .reshape(EXPERTS * SPLIT, CAP, D)
+    )
     worked = expert_rows(
         lax.all_to_all(outgoing, ("req", "wide"), split_axis=0, concat_axis=0, tiled=True),
         gate_pieces,
@@ -196,11 +217,13 @@
         down_pieces,
     )
     returned = lax.all_to_all(worked, ("req", "wide"), split_axis=0, concat_axis=0, tiled=True)
-    halves = jnp.sum(returned.reshape(EXPERTS, SPLIT, CAP, D).astype(jnp.float32), axis=1).reshape(
-        EXPERTS * CAP, D
-    )
-    picked = jnp.take(halves, target.reshape(-1), axis=0).reshape(rows, TOPK, D)
-    routed = jnp.sum(gates[..., None] * picked, axis=1)
+    weight = jnp.sum(jnp.where(match.transpose(1, 0, 2), gates[:, None, :], 0.0), axis=-1)
+    weight_hi = weight.astype(jnp.bfloat16)
+    weight_lo = (weight - weight_hi.astype(jnp.float32)).astype(jnp.bfloat16)
+    flat = returned.reshape(EXPERTS * SPLIT * CAP, D)
+    routed = jnp.dot(weight_hi, flat, preferred_element_type=jnp.float32) + jnp.dot(
+        weight_lo, flat, preferred_element_type=jnp.float32
+    )
     return ((residual + routed).astype(jnp.bfloat16), suffix_cache)
 
 

time: 498 us -> 457 us (0.918)
  waiting for transfers between devices: 104 us -> 151 us
  blocking collectives: 163 us -> 121 us
  matrix products: 94.5 us -> 57.2 us
  Pallas kernels: 0 us -> 33.6 us
  other arithmetic: 45.2 us -> 17.3 us
  local copies, waits for them, and re-layouts: 61.6 us -> 51.9 us
    all_gather x2, waiting for transfers between devices: 0.01 us -> 48.9 us  [the longest x1 46 us: on_device(): lax.all_gather(jnp.concatenate([latent, suffix_rot], axis=1), 'wide', axi...]
    all_gather x2 -> x0, blocking collectives: 43.5 us -> none  [the longest x1 24.4 us: on_device(): page_rope = lax.all_gather(prefix_rope, 'req', axis=0, tiled=True)]
    dot_general x6 -> x2, matrix products: 44.9 us -> 6.62 us  [the longest x1 4.63 us: on_device(): jnp.dot(weight_hi, flat, preferred_element_type=jnp.float32)]
    pallas_call x0 -> x1, Pallas kernels: none -> 33.6 us  [attend(): pl.pallas_call(functools.partial(attend_kernel, window=window, scale=1.0...]
    reduce_sum x4 -> x1, other arithmetic: 26.7 us -> 2.28 us  [on_device(): jnp.sum(jnp.where(match.transpose(1, 0, 2), gates[:, None, :], 0.0), axis...]
    gather x2 -> x0, local copies, waits for them, and re-layouts: 18.2 us -> none  [on_device(): picked = jnp.take(halves, target.reshape(-1), axis=0).reshape(rows, TOPK, D)]
    reshape x2, local copies, waits for them, and re-layouts: 8.31 us -> 21.6 us  [the longest x1 11.1 us: on_device(): outgoing = jnp.dot(selector, normed, preferred_element_type=jnp.float32)....]
    broadcast_in_dim x2 -> x4, local copies, waits for them, and re-layouts: 12.6 us -> 3.3 us  [the longest x2 1.66 us: on_device(): hi = jnp.repeat(index_q[:, None], HEADS, axis=0)]
  transfers between devices with their start and end apart: 3 -> 3, of which waited for: 1 -> 3; matrix products, arithmetic and copies ran while one was open for 9% -> 7% of each run, Pallas kernels for 0% -> 0%
where the time goes in v1:
time: 457 us; the launch traced here: 453 us
  waiting for transfers between devices  151 us (33%)
  blocking collectives  121 us (26%)
  matrix products  57.2 us (13%)
  local copies, waits for them, and re-layouts  51.9 us (11%)
  Pallas kernels  33.6 us (7%)
  other arithmetic  17.3 us (4%)
  between operations  15.2 us (3%)
  starting transfers between devices  5.92 us (1%)
    all_to_all x1, blocking collectives, on_device(): lax.all_to_all(outgoing, ('req', 'wide'), split_axis=0, concat_axis=0, ti...  106 us
    all_to_all x1, waiting for transfers between devices, on_device(): lax.all_to_all(worked, ('req', 'wide'), split_axis=0, concat_axis=0, tile...  102 us
    all_gather x1, waiting for transfers between devices, on_device(): lax.all_gather(jnp.concatenate([latent, suffix_rot], axis=1), 'wide', axi...  46 us
    pallas_call x1, Pallas kernels, attend(): pl.pallas_call(functools.partial(attend_kernel, window=window, scale=1.0...  33.6 us
    all_gather x1, blocking collectives, on_device(): group_seg = lax.all_gather(segment_ids, 'wide', axis=1, tiled=True)[0]  15.2 us
    reshape x1, local copies, waits for them, and re-layouts, on_device(): outgoing = jnp.dot(selector, normed, preferred_element_type=jnp.float32)....  11.1 us
    dot_general x1, matrix products, expert_rows(): jnp.einsum('spkd,pdf->spkf', grid, gate_pieces, preferred_element_type=jn...  11.1 us
    dot_general x1, matrix products, expert_rows(): jnp.einsum('spkd,pdf->spkf', grid, up_pieces, preferred_element_type=jnp....  10.7 us
  transfers between devices with their start and end apart: 3, of which 3 were waited for; matrix products, arithmetic and copies ran while one was open for 7% of the time, Pallas kernels for 0%

profile of v1, /device:TPU:5, one launch (start us, length us, event | category | flops | bytes accessed | tf_op | source)
XLA Modules:
  0.0 453.3 jit_solution(17571647139762293234)
XLA Ops:
  7.3 2.8 fusion.50
  10.2 15.2 %all_gather.9 = s32[1,2048]{1,0:T(1,128)S(1)} all-gather(s32[1,128]{1,0:T(1,128)} %param.32), channel_id=1, replica_groups=mesh['req'=8,'wide'=16] {'wide'}, dimensions={1}, use_global_device_ids=true | all-gather | bytes 8704 | tf_op jit(solution)/shard_map/all_gather | solution.py:151
  25.5 0.3 reduce-window.15
  26.1 0.8 copy.116
  27.0 1.3 fusion.46
  29.0 1.2 subtract_convert_fusion.3
  30.2 1.7 pad_maximum_fusion.1
  31.9 0.1 copy.134
  32.3 1.6 pad_maximum_fusion.3
  34.0 0.1 eq.83
  34.1 0.1 eq.87
  34.3 3.9 copy.132
  38.2 2.3 copy.109
  40.7 1.0 slice_convert_fusion
  41.8 2.4 convert_bitcast_fusion
  44.1 1.6 pad_maximum_fusion
  45.8 4.9 %copy.115 = bf16[128,16,576]{2,1,0:T(8,128)(2,1)} copy(bf16[128,16,576]{0,2,1:T(8,128)(2,1)} %pad_maximum_fusion) | data formatting | bytes 4718592 | tf_op jit(solution)/shard_map/concatenate | solution.py:171
  50.8 1.6 broadcast_in_dim.78.lo_ref
  52.4 1.6 broadcast_in_dim.79.hi_ref
  54.0 1.8 reduce-window.19
  55.8 0.3 slice_reduce_fusion
  56.1 0.1 fusion.34
  56.3 0.1 reshape.238
  56.5 3.6 fusion.6
  60.1 2.9 all-gather.3.cloned.1.call-done.kp_ref
  63.0 46.0 %all-gather.5.cloned.1.call-done.ks_ref = bf16[2048,576]{1,0:T(8,128)(2,1)} async-done(((bf16[128,576]{1,0:T(8,128)(2,1)}), bf16[2048,576]{1,0:T(8,128)(2,1)}) %all-gather.5.cloned.1.call-update) | async-done | bytes 2359312 | tf_op jit(solution)/shard_map/all_gather | solution.py:160
  109.0 33.6 %shard_map.176 = bf16[2048,512]{1,0:T(8,128)(2,1)} custom-call(s32[1]{0:T(128)} %bitcast.base_ref, bf16[2048,576]{1,0:T(8,128)(2,1)} %bitcast.104, bf16[1024,576]{1,0:T(8,128)(2,1)} %all-gather.3.cloned.1.call-done.kp_ref, bf16[2048,576]{1,0:T(8,128)(2,1)} %all-gather.5.cloned.1.call-done.ks_ref, s32[2048,1]{1,0:T(8,128)} %broadcast_in_dim.78.lo_ref, ...), custom_call_target="tpu_custom_call" | custom-call | tf_op jit(solution)/shard_map/pallas_call | solution.py:90
  142.6 3.8 fusion.25
  146.4 4.8 %multiply_reduce_fusion = (f32[128]{0:T(128)S(1)}, f32[128,2048]{1,0:T(8,128)S(1)}) fusion(bf16[128,2048]{0,1:T(8,128)(2,1)S(1)} %bitcast.109, bf16[2048,2048]{1,0:T(8,128)(2,1)} %param.23, bf16[128,2048]{1,0:T(8,128)(2,1)S(1)} %copy-done.5), kind=kOutput, calls=%fused_computation.38 | convolution fusion | flops 1074790272 | bytes 10486272 | tf_op jit(solution)/shard_map/dot_general | solution.py:190
  151.2 1.0 copy-done.3
  152.2 5.1 %convolution_convert_fusion = bf16[1792,2048]{1,0:T(8,128)(2,1)} fusion(pred[1792,128]{1,0:T(8,128)(4,1)S(1)} %fusion.6, f32[128,2048]{1,0:T(8,128)S(1)} %get-tuple-element.29, f32[2048]{0:T(1024)S(1)} %copy-done.9, f32[128]{0:T(128)S(1)} %add_rsqrt_fusion), kind=kOutput, calls=%fused_computation | convolution fusion | flops 943980544 | bytes 8626688 | tf_op jit(solution)/shard_map/dot_general | solution.py:209
  157.3 11.1 %reshape.239 = bf16[128,14,2048]{2,1,0:T(8,128)(2,1)} reshape(bf16[1792,2048]{1,0:T(8,128)(2,1)} %convolution_convert_fusion) | data formatting | bytes 14680064 | tf_op jit(solution)/shard_map/reshape | solution.py:211
  168.4 106.2 %all_to_all.10 = bf16[128,14,2048]{2,1,0:T(8,128)(2,1)S(1)} all-to-all(bf16[128,14,2048]{2,1,0:T(8,128)(2,1)} %reshape.239), channel_id=1, replica_groups=mesh['req'=8,'wide'=16] {'req','wide'}, dimensions={0} | all-to-all | bytes 14680064 | tf_op jit(solution)/shard_map/all_to_all | solution.py:214
  274.6 10.7 %fusion = f32[128,14,704]{0,2,1:T(8,128)S(1)} fusion(bf16[128,14,2048]{2,1,0:T(8,128)(2,1)S(1)} %all_to_all.10, bf16[1,2048,704]{1,2,0:T(8,128)(2,1)S(1)} %copy-done.11), kind=kOutput, calls=%fused_computation.1 | convolution fusion | flops 5167382528 | bytes 15269888 | tf_op jit(solution)/shard_map/spkd,pdf->spkf/dot_general | solution.py:112
  285.4 11.1 %fusion.2 = f32[128,14,704]{0,2,1:T(8,128)S(1)} fusion(bf16[128,14,2048]{2,1,0:T(8,128)(2,1)S(1)} %all_to_all.10, bf16[1,2048,704]{1,2,0:T(8,128)(2,1)S(1)} %copy-done.12), kind=kOutput, calls=%fused_computation.3 | convolution fusion | flops 5167382528 | bytes 15269888 | tf_op jit(solution)/shard_map/spkd,pdf->spkf/dot_general | solution.py:111
  296.5 8.4 %convolution_convert_fusion.1 = bf16[128,14,2048]{2,0,1:T(8,128)(2,1)} fusion(bf16[1,704,2048]{2,1,0:T(8,128)(2,1)S(1)} %copy-done, f32[128,14,704]{0,2,1:T(8,128)S(1)} %fusion, f32[128,14,704]{0,2,1:T(8,128)S(1)} %fusion.2), kind=kOutput, calls=%fused_computation.20 | convolution fusion | flops 5178621952 | bytes 20316160 | tf_op jit(solution)/shard_map/spkf,pfd->spkd/dot_general | solution.py:114
  304.8 10.4 %copy.130 = bf16[128,14,2048]{2,1,0:T(8,128)(2,1)} copy(bf16[128,14,2048]{2,0,1:T(8,128)(2,1)} %convolution_convert_fusion.1) | data formatting | bytes 14680064 | tf_op jit(solution)/shard_map/convert_element_type | solution.py:116
  315.2 5.8 %all-to-all-start.1 = ((bf16[128,14,2048]{2,1,0:T(8,128)(2,1)}), bf16[128,14,2048]{2,1,0:T(8,128)(2,1)}, u32[]{:S(2)}, u32[]{:S(2)}) async-start(bf16[128,14,2048]{2,1,0:T(8,128)(2,1)} %copy.130), calls=%async_computation.1 | async-start | bytes 16777216 | tf_op jit(solution)/shard_map/all_to_all | solution.py:219
  321.1 0.8 copy.131
  321.9 1.6 fusion.49
  323.6 2.3 select_reduce_fusion
  325.8 102.0 %all-to-all-done.1 = bf16[128,14,2048]{2,1,0:T(8,128)(2,1)} async-done(((bf16[128,14,2048]{2,1,0:T(8,128)(2,1)}), bf16[128,14,2048]{2,1,0:T(8,128)(2,1)}, u32[]{:S(2)}, u32[]{:S(2)}) %all-to-all-start.1) | async-done | bytes 7340064 | tf_op jit(solution)/shard_map/all_to_all | solution.py:219
  427.8 10.5 %reshape.244 = bf16[1792,2048]{1,0:T(8,128)(2,1)} reshape(bf16[128,14,2048]{2,1,0:T(8,128)(2,1)} %all-to-all-done.1) | data formatting | bytes 14680064 | tf_op jit(solution)/shard_map/reshape | solution.py:223
  438.3 4.6 %fusion.30 = f32[128,2048]{1,0:T(8,128)S(1)} fusion(bf16[1792,2048]{1,0:T(8,128)(2,1)} %reshape.244, f32[128,1792]{1,0:T(8,128)} %select_reduce_fusion), kind=kOutput, calls=%fused_computation.47 | convolution fusion | flops 939753472 | bytes 9306112 | tf_op jit(solution)/shard_map/dot_general | solution.py:224
  443.0 0.8 copy-done.1
  443.8 0.2 copy-done.2
  444.0 0.3 copy-done.4
  444.3 2.0 fusion.17
  (58 shorter events, 1.8 us)
Async XLA Ops:
  7.2 289.3 %copy-start = (bf16[1,704,2048]{2,1,0:T(8,128)(2,1)S(1)}, bf16[1,704,2048]{2,1,0:T(8,128)(2,1)}, u32[]{:S(2)}) copy-start(bf16[1,704,2048]{2,1,0:T(8,128)(2,1)} %param.28) | copy-start | bytes 8650756
  7.2 25.0 %copy-start.10 = (f32[512]{0:T(512)S(1)}, f32[512]{0:T(512)}, u32[]{:S(2)}) copy-start(f32[512]{0:T(512)} %param.20) | copy-start | bytes 6148
  7.2 26.7 %copy-start.8 = (s32[128,6]{0,1:T(8,128)S(1)}, s32[128,6]{0,1:T(8,128)}, u32[]{:S(2)}) copy-start(s32[128,6]{0,1:T(8,128)} %param.33) | copy-start | bytes 9220
  7.2 55.8 %all-gather.3.cloned.1.call-start = ((), (), s32[]{:S(2)}) async-start(), calls=%async_computation.2 | async-start | bytes 1474560 | tf_op jit(solution)/shard_map/all_gather | solution.py:150
  31.8 77.2 %all-gather.5.cloned.1.call-start = ((), (), s32[]{:S(2)}) async-start(), calls=%async_computation.3 | async-start | bytes 2785280 | tf_op jit(solution)/shard_map/all_gather | solution.py:160
  32.3 8.2 %copy-start.7 = (f32[128,32]{1,0:T(8,128)S(1)}, f32[128,32]{1,0:T(8,128)}, u32[]{:S(2)}) copy-start(f32[128,32]{1,0:T(8,128)} %get-tuple-element.24) | copy-start | bytes 49156
  142.6 3.8 copy-start.5
  146.4 5.8 %copy-start.9 = (f32[2048]{0:T(1024)S(1)}, f32[2048]{0:T(1024)}, u32[]{:S(2)}) copy-start(f32[2048]{0:T(1024)} %param.24) | copy-start | bytes 24580
  151.2 1.0 copy-start.3
  168.4 106.2 %copy-start.11 = (bf16[1,2048,704]{1,2,0:T(8,128)(2,1)S(1)}, bf16[1,2048,704]{1,2,0:T(8,128)(2,1)}, u32[]{:S(2)}) copy-start(bf16[1,2048,704]{1,2,0:T(8,128)(2,1)} %param.27) | copy-start | bytes 8650756
  274.6 10.7 %copy-start.12 = (bf16[1,2048,704]{1,2,0:T(8,128)(2,1)S(1)}, bf16[1,2048,704]{1,2,0:T(8,128)(2,1)}, u32[]{:S(2)}) copy-start(bf16[1,2048,704]{1,2,0:T(8,128)(2,1)} %param.26) | copy-start | bytes 8650756
  315.2 6.6 %copy-start.6 = (bf16[2048,64]{0,1:T(8,128)(2,1)S(1)}, bf16[2048,64]{0,1:T(8,128)(2,1)}, u32[]{:S(2)}) copy-start(bf16[2048,64]{0,1:T(8,128)(2,1)} %param.25) | copy-start | bytes 786436
  315.2 112.6 %all-to-all-start.1 = ((bf16[128,14,2048]{2,1,0:T(8,128)(2,1)}), bf16[128,14,2048]{2,1,0:T(8,128)(2,1)}, u32[]{:S(2)}, u32[]{:S(2)}) async-start(bf16[128,14,2048]{2,1,0:T(8,128)(2,1)} %copy.130), calls=%async_computation.1 | async-start | bytes 16777216 | tf_op jit(solution)/shard_map/all_to_all | solution.py:219
  438.3 5.4 %copy-start.1 = (bf16[1792,2048]{1,0:T(8,128)(2,1)S(1)}, bf16[1792,2048]{1,0:T(8,128)(2,1)}, u32[]{:S(2)}) copy-start(bf16[1792,2048]{1,0:T(8,128)(2,1)} %reshape.244) | copy-start | bytes 22020100
  438.3 5.6 %copy-start.2 = (f32[128,1792]{1,0:T(8,128)S(1)}, f32[128,1792]{1,0:T(8,128)}, u32[]{:S(2)}) copy-start(f32[128,1792]{1,0:T(8,128)} %select_reduce_fusion) | copy-start | bytes 2752516
  438.3 5.9 %copy-start.4 = (f32[128,2048]{1,0:T(8,128)S(1)}, f32[128,2048]{1,0:T(8,128)}, u32[]{:S(2)}) copy-start(f32[128,2048]{1,0:T(8,128)} %copy-done.3) | copy-start | bytes 3145732
Sparse Core Ops, SparseCore 0:
  32.0 30.9 all-gather.2
  65.1 43.8 all-gather.4
